TPU v7x, 512 devices: a whole 4x8x8 slice. The times are simulated.
512 devices in a mesh: ulysses: 8 (over z_hi, x), context: 64 (over y, z_lo, core).
Axes of the slice: x: 4, y: 8, z: 8 (z_hi: 2, z_lo: 4; z = z_hi * 4 + z_lo), core: 2. Of those that a mesh axis runs over, the one named last changes fastest.
Arguments:
- queries: bfloat16 [49152, 5120], P(('context', 'ulysses')), may hold values from -7 to 7
- key_vectors: bfloat16 [49152, 5120], P(('context', 'ulysses')), may hold values from -7 to 7
- value_vectors: bfloat16 [49152, 5120], P(('context', 'ulysses')), may hold values from -6 to 6
- labels: int32 [40], replicated, may hold values from 0 to 1, as said below
- block_lists: int32 [40, 768, 5], replicated, may hold values from 0 to 767, as said below
- counts: int32 [40, 768], replicated, may hold values from 1 to 5, as said below
- query_scale: float32 [40], replicated, may hold values from 1.5 to 3
- key_scale: float32 [40], replicated, may hold values from 1.5 to 3
- value_scale: float32 [40], replicated, may hold values from 0.5 to 2
Outputs:
- attended: bfloat16 [49152, 5120], P(('context', 'ulysses'))
Inputs may be any that keep to these rules, and one draw needn't show every extreme that they name: `labels`: exactly 16 entries are 1, the others 0; every aligned run of 5 heads holds at least one 0. Every entry of block_lists[h, b] lies within 2 blocks of b; the first entry is b itself and the first counts[h, b] entries are distinct. counts[h, b] is at least one less than and at most the number of blocks of the clip within 2 blocks of b; every head has a query block that uses all 5 entries.
All inputs are finite; a program needn't handle non-finite values.
Results may differ from a plain program's by a relative error of at most 0.0024.
Values may be sent and summed in bfloat16 or wider, within the bound.
No kernel may reach another device: no remote copies, remote signals or barrier semaphores. Data moves between devices by JAX's collectives and lax.ppermute only.
A program may use at most 128 MiB of HBM per device.

v0:
```python
import math
import jax
import jax.numpy as jnp
from jax import lax
from jax.sharding import Mesh, PartitionSpec as P

FRAMES = 16
MARGIN = 2
BLOCK = 64


def with_halo(cells, axes, order):
    width = MARGIN * BLOCK
    pairs = list(zip(order[:-1], order[1:]))
    lower = lax.ppermute(cells[-width:], axes, pairs)
    upper = lax.ppermute(cells[:width], axes, [(b, a) for a, b in pairs])
    return jnp.concatenate([lower, cells, upper], axis=0)


def window_mask(block_lists, counts, head_ids, base, blocks):
    span = 2 * MARGIN + 1
    list_length = block_lists.shape[2]
    head_lists = jnp.take(block_lists, head_ids, axis=0)
    head_counts = jnp.take(counts, head_ids, axis=0)
    global_ids = base[:, None] + jnp.arange(blocks, dtype=jnp.int32)[None, :]
    lists = jnp.take_along_axis(head_lists, global_ids[:, :, None], axis=1)
    used = jnp.take_along_axis(head_counts, global_ids, axis=1)
    wanted = global_ids[:, :, None] + jnp.arange(span, dtype=jnp.int32)[None, None, :] - MARGIN
    live = jnp.arange(list_length, dtype=jnp.int32)[None, None, :] < used[:, :, None]
    hit = (lists[:, :, None, :] == wanted[:, :, :, None]) & live[:, :, None, :]
    return jnp.any(hit, axis=-1)


def attend(query_rows, key_ext, value_ext, allowed, logit_scale, value_factor):
    rows, heads, width = query_rows.shape
    blocks = rows // BLOCK
    span = 2 * MARGIN + 1
    q = query_rows.reshape(blocks, BLOCK, heads, width)
    kb = key_ext.reshape(blocks + 2 * MARGIN, BLOCK, heads, width)
    vb = value_ext.reshape(blocks + 2 * MARGIN, BLOCK, heads, width)
    kw = jnp.stack([kb[o : o + blocks] for o in range(span)], axis=1)
    vw = jnp.stack([vb[o : o + blocks] for o in range(span)], axis=1)
    logits = jnp.einsum("bqhd,bokhd->hbqok", q, kw, preferred_element_type=jnp.float32)
    logits = logits * logit_scale[:, None, None, None, None]
    logits = jnp.where(allowed[:, :, None, :, None], logits, -jnp.inf)
    peak = jnp.max(logits, axis=(3, 4), keepdims=True)
    weight = jnp.exp(logits - peak)
    total = jnp.sum(weight, axis=(3, 4))
    mixed = jnp.einsum(
        "hbqok,bokhd->bqhd", weight.astype(jnp.bfloat16), vw, preferred_element_type=jnp.float32
    )
    factor = value_factor[:, None, None] / total
    out = mixed * jnp.transpose(factor, (1, 2, 0))[:, :, :, None]
    return out.astype(jnp.bfloat16).reshape(rows, heads, width)


def shards(
    queries,
    key_vectors,
    value_vectors,
    labels,
    block_lists,
    counts,
    query_scale,
    key_scale,
    value_scale,
):
    groups = lax.axis_size("ulysses")
    frames = lax.axis_size("frame")
    quarters = lax.axis_size("quarter")
    devices_along = frames * quarters
    tokens_here = queries.shape[0]
    head_count = labels.shape[0]
    width = queries.shape[1] // head_count
    per_group = head_count // groups
    rows = tokens_here * groups
    blocks = rows // BLOCK
    piece = rows // frames
    group_index = lax.axis_index("ulysses")
    frame_index = lax.axis_index("frame")
    quarter_index = lax.axis_index("quarter")
    spatial_slot = frame_index * quarters + quarter_index
    temporal_slot = quarter_index * frames + frame_index
    stacked = jnp.concatenate(
        [
            queries.reshape(tokens_here, groups, per_group, width),
            key_vectors.reshape(tokens_here, groups, per_group, width),
            value_vectors.reshape(tokens_here, groups, per_group, width),
        ],
        axis=2,
    )
    frame_rows = lax.all_to_all(stacked, "ulysses", split_axis=1, concat_axis=0, tiled=True)
    frame_rows = frame_rows.reshape(rows, 3 * per_group, width)
    moved = lax.all_to_all(
        frame_rows.reshape(frames, piece, 3 * per_group, width),
        "frame",
        split_axis=0,
        concat_axis=0,
        tiled=True,
    )
    line_rows = jnp.transpose(moved, (1, 0, 2, 3)).reshape(rows, 3 * per_group, width)
    spatial_order = list(range(devices_along))
    temporal_order = [k % frames * quarters + k // frames for k in range(devices_along)]
    frame_ext = with_halo(frame_rows[:, per_group:], ("frame", "quarter"), spatial_order)
    line_ext = with_halo(line_rows[:, per_group:], ("frame", "quarter"), temporal_order)
    head_ids = group_index * per_group + jnp.arange(per_group, dtype=jnp.int32)
    temporal = jnp.take(labels, head_ids) == 1
    doubled = jnp.concatenate([temporal, temporal])
    query_rows = jnp.where(
        temporal[None, :, None], line_rows[:, :per_group], frame_rows[:, :per_group]
    )
    extended = jnp.where(doubled[None, :, None], line_ext, frame_ext)
    base = jnp.where(temporal, temporal_slot * blocks, spatial_slot * blocks).astype(jnp.int32)
    allowed = window_mask(block_lists, counts, head_ids, base, blocks)
    logit_scale = jnp.take(query_scale, head_ids) * jnp.take(key_scale, head_ids) / math.sqrt(width)
    value_factor = jnp.take(value_scale, head_ids)
    outputs = attend(
        query_rows,
        extended[:, :per_group],
        extended[:, per_group:],
        allowed,
        logit_scale,
        value_factor,
    )
    back = jnp.transpose(outputs.reshape(piece, frames, per_group, width), (1, 0, 2, 3))
    returned = lax.all_to_all(back, "frame", split_axis=0, concat_axis=0, tiled=True)
    returned = returned.reshape(rows, per_group, width)
    frame_outputs = jnp.where(temporal[None, :, None], returned, outputs)
    merged = lax.all_to_all(
        frame_outputs.reshape(rows, 1, per_group, width),
        "ulysses",
        split_axis=0,
        concat_axis=1,
        tiled=True,
    )
    return merged.reshape(tokens_here, head_count * width)


def solution(mesh):
    ulysses, context = mesh.devices.shape
    fine = Mesh(
        mesh.devices.reshape(ulysses, FRAMES, context // FRAMES), ("ulysses", "frame", "quarter")
    )
    rows = P(("frame", "quarter", "ulysses"), None)
    placed = (rows, rows, rows, P(), P(), P(), P(), P(), P())
    return jax.shard_map(shards, mesh=fine, in_specs=placed, out_specs=rows, check_vma=False)
```

profile of v0, /device:TPU:48, one launch (start us, length us, event | category | flops | bytes accessed | tf_op | source)
XLA Modules:
  0.0 332.7 jit_solution(10874801442408721896)
XLA Ops:
  0.0 1.8 copy.74
  1.8 1.7 copy.75
  3.5 2.4 copy.76
  5.9 3.4 %pad_maximum_fusion = bf16[96,8,15,128]{0,3,2,1:T(8,128)(2,1)} fusion(bf16[96,8,5,128]{0,3,2,1:T(8,128)(2,1)} %bitcast.67, bf16[96,8,5,128]{0,3,2,1:T(8,128)(2,1)S(1)} %bitcast.66, bf16[96,8,5,128]{0,3,2,1:T(8,128)(2,1)S(1)} %bitcast.65), kind=kLoop, calls=%fused_computation.16 | loop fusion | flops 2949120 | bytes 5898240 | tf_op jit(solution)/shard_map/concatenate | solution.py:84
  9.3 5.8 %copy.77 = bf16[96,8,15,128]{3,0,2,1:T(8,128)(2,1)} copy(bf16[96,8,15,128]{0,3,2,1:T(8,128)(2,1)} %pad_maximum_fusion) | data formatting | bytes 5898240 | tf_op jit(solution)/shard_map/concatenate | solution.py:84
  15.0 82.2 %all_to_all.40 = bf16[96,8,15,128]{3,0,2,1:T(8,128)(2,1)S(1)} all-to-all(bf16[96,8,15,128]{3,0,2,1:T(8,128)(2,1)} %copy.77), channel_id=1, replica_groups=mesh['ulysses'=8,'frame'=16,'quarter'=4] {'ulysses'}, dimensions={1} | all-to-all | bytes 5898240 | tf_op jit(solution)/shard_map/all_to_all | solution.py:92
  97.2 0.3 copy.78
  97.5 1.6 copy-done.6
  99.1 2.2 copy.79
  101.3 11.1 %all-to-all-start.1 = ((bf16[16,48,15,128]{3,1,2,0:T(8,128)(2,1)}), bf16[16,48,15,128]{3,1,2,0:T(8,128)(2,1)}, u32[]{:S(2)}, u32[]{:S(2)}) async-start(bf16[16,48,15,128]{3,1,2,0:T(8,128)(2,1)} %copy.79), calls=%async_computation.1 | async-start | bytes 5898240 | tf_op jit(solution)/shard_map/all_to_all | solution.py:94
  112.4 0.6 gather_fusion.7
  113.0 0.6 gather_fusion.6
  113.7 0.6 gather_fusion.5
  114.4 0.6 gather_fusion
  115.2 0.6 gather_fusion.2
  115.8 1.0 gather_fusion.4
  116.9 0.7 gather_fusion.1
  117.7 0.6 copy.86
  118.3 1.1 gather_fusion.3
  119.8 1.1 fusion.16
  121.0 1.9 collective-permute-start.2
  122.9 6.3 %collective-permute-start.3 = (bf16[128,10,128]{2,0,1:T(8,128)(2,1)S(1)}, bf16[128,10,128]{2,0,1:T(8,128)(2,1)S(1)}, u32[]{:S(2)}, u32[]{:S(2)}) collective-permute-start(bf16[128,10,128]{2,0,1:T(8,128)(2,1)S(1)} %get-tuple-element.11), channel_id=1, source_target_pairs={{1,0},{2,1},{3,2},{4,3},{5,4},{6,5},{7,6},{8,7},{9,8},{10,9},{11,1... | collective-permute-start | bytes 983048 | tf_op jit(solution)/shard_map/ppermute | solution.py:16
  129.2 82.6 %all-to-all-done.1 = bf16[16,48,15,128]{3,1,2,0:T(8,128)(2,1)} async-done(((bf16[16,48,15,128]{3,1,2,0:T(8,128)(2,1)}), bf16[16,48,15,128]{3,1,2,0:T(8,128)(2,1)}, u32[]{:S(2)}, u32[]{:S(2)}) %all-to-all-start.1) | async-done | bytes 2949152 | tf_op jit(solution)/shard_map/all_to_all | solution.py:94
  211.8 2.6 copy.80
  214.4 1.6 copy-done.7
  216.1 1.9 collective-permute-start
  218.0 5.9 %collective-permute-start.1 = (bf16[128,10,128]{2,0,1:T(8,128)(2,1)S(1)}, bf16[128,10,128]{2,0,1:T(8,128)(2,1)S(1)}, u32[]{:S(2)}, u32[]{:S(2)}) collective-permute-start(bf16[128,10,128]{2,0,1:T(8,128)(2,1)S(1)} %get-tuple-element.13), channel_id=1, source_target_pairs={{4,0},{8,4},{12,8},{16,12},{20,16},{24,20},{28,24},{32,28},{36,32}... | collective-permute-start | bytes 983048 | tf_op jit(solution)/shard_map/ppermute | solution.py:16
  224.0 0.1 copy.89
  224.1 1.9 slice.118
  226.0 0.6 copy-done.8
  226.6 0.1 slice.115
  226.7 1.4 slice_select_fusion
  228.1 6.4 %collective-permute-done = bf16[128,10,128]{2,0,1:T(8,128)(2,1)S(1)} collective-permute-done((bf16[128,10,128]{2,0,1:T(8,128)(2,1)S(1)}, bf16[128,10,128]{2,0,1:T(8,128)(2,1)S(1)}, u32[]{:S(2)}, u32[]{:S(2)}) %collective-permute-start) | collective-permute-done | bytes 327712 | tf_op jit(solution)/shard_map/ppermute | solution.py:15
  234.5 11.7 %collective-permute-done.1 = bf16[128,10,128]{2,0,1:T(8,128)(2,1)S(1)} collective-permute-done((bf16[128,10,128]{2,0,1:T(8,128)(2,1)S(1)}, bf16[128,10,128]{2,0,1:T(8,128)(2,1)S(1)}, u32[]{:S(2)}, u32[]{:S(2)}) %collective-permute-start.1) | collective-permute-done | bytes 327712 | tf_op jit(solution)/shard_map/ppermute | solution.py:16
  246.2 0.8 maximum_select_fusion
  247.1 0.8 fusion.18
  248.3 0.1 constant_dynamic-update-slice_fusion.6
  248.5 1.5 fusion
  250.1 3.0 fusion.1
  253.8 2.1 fusion.6
  255.9 0.3 copy.93
  256.2 31.2 %all_to_all.41 = bf16[16,48,5,128]{3,1,2,0:T(8,128)(2,1)S(1)} all-to-all(bf16[16,48,5,128]{3,1,2,0:T(8,128)(2,1)S(1)} %copy.93), channel_id=1, replica_groups=mesh['ulysses'=8,'frame'=16,'quarter'=4] {'frame'}, dimensions={0} | all-to-all | bytes 1966080 | tf_op jit(solution)/shard_map/all_to_all | solution.py:126
  287.5 0.2 bitcast_select_fusion
  287.7 0.7 copy.96
  288.5 42.0 %all_to_all.42 = bf16[768,1,5,128]{3,2,1,0:T(8,128)(2,1)S(1)} all-to-all(bf16[768,1,5,128]{3,2,1,0:T(8,128)(2,1)S(1)} %copy.96), channel_id=1, replica_groups=mesh['ulysses'=8,'frame'=16,'quarter'=4] {'ulysses'}, dimensions={0} | all-to-all | bytes 1966080 | tf_op jit(solution)/shard_map/all_to_all | solution.py:129
  330.5 0.1 copy.97
  330.6 0.8 copy.98
  331.4 1.4 copy.99
  (55 shorter events, 2.3 us)
Async XLA Ops:
  0.0 116.9 %copy-start = (s32[40,768,5]{1,0,2:T(8,128)S(1)}, s32[40,768,5]{1,0,2:T(8,128)}, u32[]{:S(2)}) copy-start(s32[40,768,5]{1,0,2:T(8,128)} %param.15) | copy-start | bytes 1843204
  97.5 1.6 copy-start.6
  99.1 13.3 %copy-start.2 = (f32[40]{0:T(128)S(1)}, f32[40]{0:T(128)}, u32[]{:S(2)}) copy-start(f32[40]{0:T(128)} %param.19) | copy-start | bytes 484
  99.1 13.9 %copy-start.3 = (f32[40]{0:T(128)S(1)}, f32[40]{0:T(128)}, u32[]{:S(2)}) copy-start(f32[40]{0:T(128)} %param.18) | copy-start | bytes 484
  101.3 12.4 %copy-start.4 = (f32[40]{0:T(128)S(1)}, f32[40]{0:T(128)}, u32[]{:S(2)}) copy-start(f32[40]{0:T(128)} %param.17) | copy-start | bytes 484
  101.3 13.1 %copy-start.5 = (s32[40]{0:T(128)S(1)}, s32[40]{0:T(128)}, u32[]{:S(2)}) copy-start(s32[40]{0:T(128)} %param.14) | copy-start | bytes 484
  101.3 13.9 %copy-start.9 = (s32[40,768]{1,0:T(8,128)S(1)}, s32[40,768]{1,0:T(8,128)}, u32[]{:S(2)}) copy-start(s32[40,768]{1,0:T(8,128)} %param.16) | copy-start | bytes 368644
  101.3 110.5 %all-to-all-start.1 = ((bf16[16,48,15,128]{3,1,2,0:T(8,128)(2,1)}), bf16[16,48,15,128]{3,1,2,0:T(8,128)(2,1)}, u32[]{:S(2)}, u32[]{:S(2)}) async-start(bf16[16,48,15,128]{3,1,2,0:T(8,128)(2,1)} %copy.79), calls=%async_computation.1 | async-start | bytes 5898240 | tf_op jit(solution)/shard_map/all_to_all | solution.py:94
  121.0 107.1 %collective-permute-start.2 = (bf16[128,10,128]{2,0,1:T(8,128)(2,1)S(1)}, bf16[128,10,128]{2,0,1:T(8,128)(2,1)S(1)}, u32[]{:S(2)}, u32[]{:S(2)}) collective-permute-start(bf16[128,10,128]{2,0,1:T(8,128)(2,1)S(1)} %get-tuple-element.10), channel_id=1, source_target_pairs={{0,1},{1,2},{2,3},{3,4},{4,5},{5,6},{6,7},{7,8},{8,9},{9,10},{10,1... | collective-permute-start | bytes 983048 | tf_op jit(solution)/shard_map/ppermute | solution.py:15
  122.9 105.2 %collective-permute-start.3 = (bf16[128,10,128]{2,0,1:T(8,128)(2,1)S(1)}, bf16[128,10,128]{2,0,1:T(8,128)(2,1)S(1)}, u32[]{:S(2)}, u32[]{:S(2)}) collective-permute-start(bf16[128,10,128]{2,0,1:T(8,128)(2,1)S(1)} %get-tuple-element.11), channel_id=1, source_target_pairs={{1,0},{2,1},{3,2},{4,3},{5,4},{6,5},{7,6},{8,7},{9,8},{10,9},{11,1... | collective-permute-start | bytes 983048 | tf_op jit(solution)/shard_map/ppermute | solution.py:16
  214.4 1.6 copy-start.7
  216.1 18.4 %collective-permute-start = (bf16[128,10,128]{2,0,1:T(8,128)(2,1)S(1)}, bf16[128,10,128]{2,0,1:T(8,128)(2,1)S(1)}, u32[]{:S(2)}, u32[]{:S(2)}) collective-permute-start(bf16[128,10,128]{2,0,1:T(8,128)(2,1)S(1)} %get-tuple-element.12), channel_id=1, source_target_pairs={{0,4},{4,8},{8,12},{12,16},{16,20},{20,24},{24,28},{28,32},{32,36}... | collective-permute-start | bytes 983048 | tf_op jit(solution)/shard_map/ppermute | solution.py:15
  218.0 28.2 %collective-permute-start.1 = (bf16[128,10,128]{2,0,1:T(8,128)(2,1)S(1)}, bf16[128,10,128]{2,0,1:T(8,128)(2,1)S(1)}, u32[]{:S(2)}, u32[]{:S(2)}) collective-permute-start(bf16[128,10,128]{2,0,1:T(8,128)(2,1)S(1)} %get-tuple-element.13), channel_id=1, source_target_pairs={{4,0},{8,4},{12,8},{16,12},{20,16},{24,20},{28,24},{32,28},{36,32}... | collective-permute-start | bytes 983048 | tf_op jit(solution)/shard_map/ppermute | solution.py:16
  224.1 2.4 copy-start.8
  287.7 45.0 %copy-start.1 = (s32[40,768,5]{1,0,2:T(8,128)S(1)}, s32[40,768,5]{1,0,2:T(8,128)}, u32[]{:S(2)}) copy-start(s32[40,768,5]{1,0,2:T(8,128)} %param.15) | copy-start | bytes 1843204
where the time goes:
time: 333 us
  blocking collectives  155 us (47%)
  waiting for transfers between devices  101 us (30%)
  local copies, waits for them, and re-layouts  36 us (11%)
  starting transfers between devices  27.2 us (8%)
  other arithmetic  9.46 us (3%)
  matrix products  3.6 us (1%)
    all_to_all x1, waiting for transfers between devices, shards(): lax.all_to_all(frame_rows.reshape(frames, piece, 3 * per_group, width), '...  82.6 us
    all_to_all x1, blocking collectives, shards(): lax.all_to_all(stacked, 'ulysses', split_axis=1, concat_axis=0, tiled=True)  82.2 us
    all_to_all x1, blocking collectives, shards(): lax.all_to_all(frame_outputs.reshape(rows, 1, per_group, width), 'ulysses...  42 us
    all_to_all x1, blocking collectives, shards(): lax.all_to_all(back, 'frame', split_axis=0, concat_axis=0, tiled=True)  31.2 us
    ppermute x2, starting transfers between devices, with_halo(): upper = lax.ppermute(cells[:width], axes, [(b, a) for a, b in pairs])  12.2 us
    ppermute x2, waiting for transfers between devices, with_halo(): upper = lax.ppermute(cells[:width], axes, [(b, a) for a, b in pairs])  11.7 us
    all_to_all x1, starting transfers between devices, shards(): lax.all_to_all(frame_rows.reshape(frames, piece, 3 * per_group, width), '...  11.1 us
    unnamed x31, local copies, waits for them, and re-layouts  10.6 us
  transfers between devices with their start and end apart: 5, of which 3 were waited for; matrix products, arithmetic and copies ran while one was open for 4% of the time, Pallas kernels for 0%

commit v1 on v0

--- a/solution.py
+++ b/solution.py
@@ -126,12 +126,20 @@
     returned = lax.all_to_all(back, "frame", split_axis=0, concat_axis=0, tiled=True)
     returned = returned.reshape(rows, per_group, width)
     frame_outputs = jnp.where(temporal[None, :, None], returned, outputs)
-    merged = lax.all_to_all(
-        frame_outputs.reshape(rows, 1, per_group, width),
-        "ulysses",
-        split_axis=0,
-        concat_axis=1,
-        tiled=True,
+    merged = jnp.concatenate(
+        lax.all_to_all(
+            jnp.stack(
+                jnp.split(
+                    frame_outputs.reshape(rows, 1, per_group, width),
+                    lax.axis_size("ulysses"),
+                    axis=0,
+                )
+            ),
+            "ulysses",
+            0,
+            0,
+        ),
+        axis=1,
     )
     return merged.reshape(tokens_here, head_count * width)
 

time: 333 us -> 320 us (0.961)
  the two profiles are of different devices: /device:TPU:48 before, /device:TPU:128 now
where the time goes in v1:
time: 320 us; the launch traced here: 319 us
  blocking collectives  154 us (48%)
  waiting for transfers between devices  94.2 us (29%)
  local copies, waits for them, and re-layouts  35.3 us (11%)
  starting transfers between devices  22.1 us (7%)
  other arithmetic  9.46 us (3%)
  matrix products  3.6 us (1%)
    all_to_all x1, blocking collectives, shards(): lax.all_to_all(stacked, 'ulysses', split_axis=1, concat_axis=0, tiled=True)  82.5 us
    all_to_all x1, waiting for transfers between devices, shards(): lax.all_to_all(frame_rows.reshape(frames, piece, 3 * per_group, width), '...  76.7 us
    all_to_all x1, blocking collectives, shards(): lax.all_to_all(back, 'frame', split_axis=0, concat_axis=0, tiled=True)  41.4 us
    all_to_all x1, blocking collectives, shards(): lax.all_to_all(jnp.stack(jnp.split(frame_outputs.reshape(rows, 1, per_gro...  30.3 us
    unnamed x38, local copies, waits for them, and re-layouts  10.7 us
    ppermute x2, waiting for transfers between devices, with_halo(): lower = lax.ppermute(cells[-width:], axes, pairs)  10.6 us
    all_to_all x1, starting transfers between devices, shards(): lax.all_to_all(frame_rows.reshape(frames, piece, 3 * per_group, width), '...  9.61 us
    ppermute x2, starting transfers between devices, with_halo(): upper = lax.ppermute(cells[:width], axes, [(b, a) for a, b in pairs])  8.66 us
  transfers between devices with their start and end apart: 5, of which 3 were waited for; matrix products, arithmetic and copies ran while one was open for 5% of the time, Pallas kernels for 0%

profile of v1, /device:TPU:128, one launch (start us, length us, event | category | flops | bytes accessed | tf_op | source)
XLA Modules:
  0.0 319.3 jit_solution(8594840234909292795)
XLA Ops:
  0.0 1.8 copy.74
  1.8 1.7 copy.75
  3.5 2.4 copy.76
  5.9 3.4 %pad_maximum_fusion = bf16[96,8,15,128]{0,3,2,1:T(8,128)(2,1)} fusion(bf16[96,8,5,128]{0,3,2,1:T(8,128)(2,1)} %bitcast.97, bf16[96,8,5,128]{0,3,2,1:T(8,128)(2,1)S(1)} %bitcast.96, bf16[96,8,5,128]{0,3,2,1:T(8,128)(2,1)S(1)} %bitcast.95), kind=kLoop, calls=%fused_computation.16 | loop fusion | flops 2949120 | bytes 5898240 | tf_op jit(solution)/shard_map/concatenate | solution.py:84
  9.3 5.8 %copy.77 = bf16[96,8,15,128]{3,0,2,1:T(8,128)(2,1)} copy(bf16[96,8,15,128]{0,3,2,1:T(8,128)(2,1)} %pad_maximum_fusion) | data formatting | bytes 5898240 | tf_op jit(solution)/shard_map/concatenate | solution.py:84
  15.0 82.5 %all_to_all.30 = bf16[96,8,15,128]{3,0,2,1:T(8,128)(2,1)S(1)} all-to-all(bf16[96,8,15,128]{3,0,2,1:T(8,128)(2,1)} %copy.77), channel_id=1, replica_groups=mesh['ulysses'=8,'frame'=16,'quarter'=4] {'ulysses'}, dimensions={1} | all-to-all | bytes 5898240 | tf_op jit(solution)/shard_map/all_to_all | solution.py:92
  97.5 0.3 copy.78
  97.8 1.6 copy-done.6
  99.4 2.2 copy.79
  101.6 9.6 %all-to-all-start.1 = ((bf16[16,48,15,128]{3,1,2,0:T(8,128)(2,1)}), bf16[16,48,15,128]{3,1,2,0:T(8,128)(2,1)}, u32[]{:S(2)}, u32[]{:S(2)}) async-start(bf16[16,48,15,128]{3,1,2,0:T(8,128)(2,1)} %copy.79), calls=%async_computation.1 | async-start | bytes 5898240 | tf_op jit(solution)/shard_map/all_to_all | solution.py:94
  111.2 0.6 gather_fusion.7
  111.9 0.6 gather_fusion.6
  112.5 0.6 gather_fusion.5
  113.2 0.6 gather_fusion
  114.0 0.6 gather_fusion.2
  114.7 1.0 gather_fusion.4
  115.7 0.7 gather_fusion.1
  116.5 0.6 copy.86
  117.2 1.1 gather_fusion.3
  118.7 1.1 fusion.24
  119.8 1.9 collective-permute-start.2
  121.7 3.6 %collective-permute-start.3 = (bf16[128,10,128]{2,0,1:T(8,128)(2,1)S(1)}, bf16[128,10,128]{2,0,1:T(8,128)(2,1)S(1)}, u32[]{:S(2)}, u32[]{:S(2)}) collective-permute-start(bf16[128,10,128]{2,0,1:T(8,128)(2,1)S(1)} %get-tuple-element.11), channel_id=1, source_target_pairs={{1,0},{2,1},{3,2},{4,3},{5,4},{6,5},{7,6},{8,7},{9,8},{10,9},{11,1... | collective-permute-start | bytes 983048 | tf_op jit(solution)/shard_map/ppermute | solution.py:16
  125.4 76.7 %all-to-all-done.1 = bf16[16,48,15,128]{3,1,2,0:T(8,128)(2,1)} async-done(((bf16[16,48,15,128]{3,1,2,0:T(8,128)(2,1)}), bf16[16,48,15,128]{3,1,2,0:T(8,128)(2,1)}, u32[]{:S(2)}, u32[]{:S(2)}) %all-to-all-start.1) | async-done | bytes 2949152 | tf_op jit(solution)/shard_map/all_to_all | solution.py:94
  202.1 2.6 copy.80
  204.7 1.6 copy-done.7
  206.3 1.9 collective-permute-start
  208.2 5.0 %collective-permute-start.1 = (bf16[128,10,128]{2,0,1:T(8,128)(2,1)S(1)}, bf16[128,10,128]{2,0,1:T(8,128)(2,1)S(1)}, u32[]{:S(2)}, u32[]{:S(2)}) collective-permute-start(bf16[128,10,128]{2,0,1:T(8,128)(2,1)S(1)} %get-tuple-element.13), channel_id=1, source_target_pairs={{4,0},{8,4},{12,8},{16,12},{20,16},{24,20},{28,24},{32,28},{36,32}... | collective-permute-start | bytes 983048 | tf_op jit(solution)/shard_map/ppermute | solution.py:16
  213.3 0.1 copy.89
  213.5 1.9 slice.126
  215.3 0.6 copy-done.8
  215.9 0.1 slice.123
  216.0 1.4 slice_select_fusion
  217.4 10.6 %collective-permute-done = bf16[128,10,128]{2,0,1:T(8,128)(2,1)S(1)} collective-permute-done((bf16[128,10,128]{2,0,1:T(8,128)(2,1)S(1)}, bf16[128,10,128]{2,0,1:T(8,128)(2,1)S(1)}, u32[]{:S(2)}, u32[]{:S(2)}) %collective-permute-start) | collective-permute-done | bytes 327712 | tf_op jit(solution)/shard_map/ppermute | solution.py:15
  228.0 6.9 %collective-permute-done.1 = bf16[128,10,128]{2,0,1:T(8,128)(2,1)S(1)} collective-permute-done((bf16[128,10,128]{2,0,1:T(8,128)(2,1)S(1)}, bf16[128,10,128]{2,0,1:T(8,128)(2,1)S(1)}, u32[]{:S(2)}, u32[]{:S(2)}) %collective-permute-start.1) | collective-permute-done | bytes 327712 | tf_op jit(solution)/shard_map/ppermute | solution.py:16
  234.9 0.8 maximum_select_fusion
  235.8 0.8 fusion.26
  236.7 0.1 constant_dynamic-update-slice_fusion.8
  236.9 0.1 constant_dynamic-update-slice_fusion.7
  237.0 0.1 constant_dynamic-update-slice_fusion.6
  237.3 1.5 fusion
  238.8 3.0 fusion.1
  242.6 2.1 fusion.6
  244.7 0.3 copy.93
  245.0 41.4 %all_to_all.31 = bf16[16,48,5,128]{3,1,2,0:T(8,128)(2,1)S(1)} all-to-all(bf16[16,48,5,128]{3,1,2,0:T(8,128)(2,1)S(1)} %copy.93), channel_id=1, replica_groups=mesh['ulysses'=8,'frame'=16,'quarter'=4] {'frame'}, dimensions={0} | all-to-all | bytes 1966080 | tf_op jit(solution)/shard_map/all_to_all | solution.py:126
  286.4 0.2 bitcast_select_fusion
  286.9 30.3 %all_to_all.32 = bf16[8,96,1,5,128]{4,1,3,2,0:T(8,128)(2,1)S(1)} all-to-all(bf16[8,96,1,5,128]{4,1,3,2,0:T(8,128)(2,1)S(1)} %fusion.11), channel_id=1, replica_groups=mesh['ulysses'=8,'frame'=16,'quarter'=4] {'ulysses'}, dimensions={0} | all-to-all | bytes 1966080 | tf_op jit(solution)/shard_map/all_to_all | solution.py:130
  317.2 0.8 copy.96
  318.0 1.4 copy.97
  (61 shorter events, 2.2 us)
Async XLA Ops:
  0.0 115.7 %copy-start = (s32[40,768,5]{1,0,2:T(8,128)S(1)}, s32[40,768,5]{1,0,2:T(8,128)}, u32[]{:S(2)}) copy-start(s32[40,768,5]{1,0,2:T(8,128)} %param.15) | copy-start | bytes 1843204
  97.8 1.6 copy-start.6
  99.4 11.8 %copy-start.2 = (f32[40]{0:T(128)S(1)}, f32[40]{0:T(128)}, u32[]{:S(2)}) copy-start(f32[40]{0:T(128)} %param.19) | copy-start | bytes 484
  99.4 12.5 %copy-start.3 = (f32[40]{0:T(128)S(1)}, f32[40]{0:T(128)}, u32[]{:S(2)}) copy-start(f32[40]{0:T(128)} %param.18) | copy-start | bytes 484
  101.6 10.9 %copy-start.4 = (f32[40]{0:T(128)S(1)}, f32[40]{0:T(128)}, u32[]{:S(2)}) copy-start(f32[40]{0:T(128)} %param.17) | copy-start | bytes 484
  101.6 11.6 %copy-start.5 = (s32[40]{0:T(128)S(1)}, s32[40]{0:T(128)}, u32[]{:S(2)}) copy-start(s32[40]{0:T(128)} %param.14) | copy-start | bytes 484
  101.6 12.4 %copy-start.9 = (s32[40,768]{1,0:T(8,128)S(1)}, s32[40,768]{1,0:T(8,128)}, u32[]{:S(2)}) copy-start(s32[40,768]{1,0:T(8,128)} %param.16) | copy-start | bytes 368644
  101.6 100.5 %all-to-all-start.1 = ((bf16[16,48,15,128]{3,1,2,0:T(8,128)(2,1)}), bf16[16,48,15,128]{3,1,2,0:T(8,128)(2,1)}, u32[]{:S(2)}, u32[]{:S(2)}) async-start(bf16[16,48,15,128]{3,1,2,0:T(8,128)(2,1)} %copy.79), calls=%async_computation.1 | async-start | bytes 5898240 | tf_op jit(solution)/shard_map/all_to_all | solution.py:94
  119.8 97.6 %collective-permute-start.2 = (bf16[128,10,128]{2,0,1:T(8,128)(2,1)S(1)}, bf16[128,10,128]{2,0,1:T(8,128)(2,1)S(1)}, u32[]{:S(2)}, u32[]{:S(2)}) collective-permute-start(bf16[128,10,128]{2,0,1:T(8,128)(2,1)S(1)} %get-tuple-element.10), channel_id=1, source_target_pairs={{0,1},{1,2},{2,3},{3,4},{4,5},{5,6},{6,7},{7,8},{8,9},{9,10},{10,1... | collective-permute-start | bytes 983048 | tf_op jit(solution)/shard_map/ppermute | solution.py:15
  121.7 95.7 %collective-permute-start.3 = (bf16[128,10,128]{2,0,1:T(8,128)(2,1)S(1)}, bf16[128,10,128]{2,0,1:T(8,128)(2,1)S(1)}, u32[]{:S(2)}, u32[]{:S(2)}) collective-permute-start(bf16[128,10,128]{2,0,1:T(8,128)(2,1)S(1)} %get-tuple-element.11), channel_id=1, source_target_pairs={{1,0},{2,1},{3,2},{4,3},{5,4},{6,5},{7,6},{8,7},{9,8},{10,9},{11,1... | collective-permute-start | bytes 983048 | tf_op jit(solution)/shard_map/ppermute | solution.py:16
  204.7 1.6 copy-start.7
  206.3 21.7 %collective-permute-start = (bf16[128,10,128]{2,0,1:T(8,128)(2,1)S(1)}, bf16[128,10,128]{2,0,1:T(8,128)(2,1)S(1)}, u32[]{:S(2)}, u32[]{:S(2)}) collective-permute-start(bf16[128,10,128]{2,0,1:T(8,128)(2,1)S(1)} %get-tuple-element.12), channel_id=1, source_target_pairs={{0,4},{4,8},{8,12},{12,16},{16,20},{20,24},{24,28},{28,32},{32,36}... | collective-permute-start | bytes 983048 | tf_op jit(solution)/shard_map/ppermute | solution.py:15
  208.2 26.7 %collective-permute-start.1 = (bf16[128,10,128]{2,0,1:T(8,128)(2,1)S(1)}, bf16[128,10,128]{2,0,1:T(8,128)(2,1)S(1)}, u32[]{:S(2)}, u32[]{:S(2)}) collective-permute-start(bf16[128,10,128]{2,0,1:T(8,128)(2,1)S(1)} %get-tuple-element.13), channel_id=1, source_target_pairs={{4,0},{8,4},{12,8},{16,12},{20,16},{24,20},{28,24},{32,28},{36,32}... | collective-permute-start | bytes 983048 | tf_op jit(solution)/shard_map/ppermute | solution.py:16
  213.5 2.4 copy-start.8
  286.4 32.9 %copy-start.1 = (s32[40,768,5]{1,0,2:T(8,128)S(1)}, s32[40,768,5]{1,0,2:T(8,128)}, u32[]{:S(2)}) copy-start(s32[40,768,5]{1,0,2:T(8,128)} %param.15) | copy-start | bytes 1843204
